TPU v7x, 512 devices: a whole 4x8x8 slice. The times are simulated.
512 devices in a mesh: param: 32 (over x, z), ex: 16 (over y, core).
Axes of the slice: x: 4, y: 8, z: 8, core: 2. Of those that a mesh axis runs over, the one named last changes fastest.
Arguments:
- adapter_gradients: bfloat16 [512, 131072], P('ex', 'param'), may hold values from -560 to 560
- sign_hash_keys: int32 [4], replicated, may hold values from 1 to 16777215
- target_indices: int32 [256], replicated, may hold values from 0 to 511
Outputs:
- features: float32 [512, 8192], P('ex', 'param')
- scores: float32 [512, 256], P('ex')
All inputs are finite; a program needn't handle non-finite values.
Results may differ from a plain program's by a relative error of at most 0.0003.
Values sent between devices are 32-bit elements; how exact they have to be, the bound alone decides.
No kernel may reach another device: no remote copies, remote signals or barrier semaphores. Data moves between devices by JAX's collectives and lax.ppermute only.
A program may use at most 128 MiB of HBM per device.

v0:
```python
import jax
import jax.numpy as jnp
from jax import lax
from jax.sharding import Mesh, PartitionSpec as P

K = 8192
norm_eps = 1e-06


def hash_terms(sign_hash_keys, first_row, row_count, col_ids):
    mult_row = sign_hash_keys[0] | 1
    mult_col = sign_hash_keys[1] | 1
    seed_add = sign_hash_keys[2]
    row_ids = first_row + lax.iota(jnp.int32, row_count)
    return (row_ids * mult_row + seed_add, col_ids * mult_col)


def sign_block(sign_hash_keys, row_terms, col_terms):
    mix_mult = sign_hash_keys[3] | 1
    hashed = row_terms[:, None] + col_terms[None, :]
    hashed = hashed ^ lax.shift_right_logical(hashed, jnp.full_like(hashed, 16))
    hashed = hashed * mix_mult
    hashed = hashed ^ lax.shift_right_logical(hashed, jnp.full_like(hashed, 13))
    hashed = hashed * jnp.int32(-1028477387)
    hashed = hashed ^ lax.shift_right_logical(hashed, jnp.full_like(hashed, 16))
    return jnp.where(hashed < 0, jnp.bfloat16(1.0), jnp.bfloat16(-1.0))


def butterfly_sum(values, axis, count):
    distance = 1
    while distance < count:
        pairs = [(j, j ^ distance) for j in range(count)]
        values = values + lax.ppermute(values, axis, pairs)
        distance *= 2
    return values


def local(adapter_gradients, sign_hash_keys, target_indices):
    resident_example, resident_rows = adapter_gradients.shape
    row_base = lax.axis_index("param") * jnp.int32(resident_rows)
    core = lax.axis_index("ec")
    swap = [(0, 1), (1, 0)]
    turn_count = 2
    rows_per_tile = resident_rows // turn_count
    scale_k = jnp.float32(K)
    param_count = lax.psum(1, "param")
    col_width = K // param_count
    half_width = col_width // 2
    unit = ((sign_hash_keys[3] | 1) & 1).astype(jnp.float32)
    partner = lax.ppermute(adapter_gradients.astype(jnp.float32), "ec", swap) * unit
    partner = partner.astype(jnp.bfloat16)
    pair_gradients = jnp.where(
        core == 0,
        jnp.concatenate([adapter_gradients, partner], axis=0),
        jnp.concatenate([partner, adapter_gradients], axis=0),
    )
    owner = lax.iota(jnp.int32, param_count)[:, None] * col_width
    col_ids = (owner + core * half_width + lax.iota(jnp.int32, half_width)[None, :]).reshape(-1)
    row_terms, col_terms = hash_terms(sign_hash_keys, row_base, resident_rows, col_ids)
    totals = None
    for tile in range(turn_count):
        start_offset = tile * rows_per_tile
        gradient_slab = pair_gradients[:, start_offset : start_offset + rows_per_tile]
        signs = sign_block(
            sign_hash_keys, row_terms[start_offset : start_offset + rows_per_tile], col_terms
        )
        term = jnp.einsum(
            "cra,apj->pcrj",
            gradient_slab.reshape(2, resident_example, rows_per_tile),
            signs.reshape(rows_per_tile, param_count, half_width),
            preferred_element_type=jnp.float32,
        )
        totals = term if totals is None else totals + term
    blocks = totals.reshape(2 * param_count, resident_example, half_width)
    blocks = lax.all_to_all(blocks, ("param", "ec"), 0, 0, tiled=True)
    blocks = jnp.sum(blocks.reshape(param_count, 2, resident_example, half_width), axis=0)
    projected = jnp.transpose(blocks, (1, 0, 2)).reshape(resident_example, col_width)
    pool_rows = lax.all_gather(projected, ("ey", "ec"), axis=0, tiled=True)
    picks = (target_indices[:, None] == lax.iota(jnp.int32, pool_rows.shape[0])[None, :]).astype(
        jnp.float32
    )
    target_rows = jnp.dot(picks, pool_rows, precision=lax.Precision.HIGHEST)
    partial_dots = jnp.dot(projected, target_rows.T, precision=lax.Precision.HIGHEST)
    own_squares = jnp.sum(projected * projected, axis=1)
    target_squares = jnp.sum(target_rows * target_rows, axis=1)
    packed = jnp.concatenate([partial_dots.reshape(-1), own_squares, target_squares])
    packed = butterfly_sum(packed, "param", param_count)
    dot_count = partial_dots.size
    dots = packed[:dot_count].reshape(partial_dots.shape)
    total_sq = packed[dot_count : dot_count + resident_example]
    target_sq = packed[dot_count + resident_example :]
    own_scale = jnp.sqrt(scale_k / (total_sq + norm_eps))
    target_scale = jnp.sqrt(scale_k / (target_sq + norm_eps))
    features = projected * own_scale[:, None]
    scores = dots * own_scale[:, None] * target_scale[None, :] / scale_k
    return (features, scores)


def solution(mesh):
    devices = mesh.devices
    pair_mesh = Mesh(
        devices.reshape(devices.shape[0], devices.shape[1] // 2, 2), ("param", "ey", "ec")
    )
    return jax.shard_map(
        local,
        mesh=pair_mesh,
        in_specs=(P(("ey", "ec"), "param"), P(), P()),
        out_specs=(P(("ey", "ec"), "param"), P(("ey", "ec"), None)),
        check_vma=False,
    )
```

profile of v0, /device:TPU:2, one launch (start us, length us, event | category | flops | bytes accessed | tf_op | source)
XLA Modules:
  0.0 132.4 jit_solution(819672193502317939)
XLA Ops:
  0.6 0.0 copy-start
  0.6 1.1 convert_element_type.10
  1.7 1.9 %collective-permute-start = (f32[32,4096]{1,0:T(8,128)S(1)}, f32[32,4096]{1,0:T(8,128)S(1)}, u32[]{:S(2)}, u32[]{:S(2)}) collective-permute-start(f32[32,4096]{1,0:T(8,128)S(1)} %convert_element_type.10), channel_id=1, source_target_pairs={{0,1},{1,0},{2,3},{3,2},{4,5},{5,4},{6,7},{7,6},{8,9},{9,8},{10,11... | collective-permute-start | bytes 1572872 | tf_op jit(solution)/shard_map/ppermute | solution.py:50
  3.6 1.5 %fusion.42 = (s32[1]{0:T(128)}, s32[1]{0:T(128)}, s32[1]{0:T(128)}, s32[1]{0:T(128)}) fusion(s32[4]{0:T(128)} %param.4), kind=kLoop, calls=%fused_computation.58 | loop fusion | bytes 32 | tf_op jit(solution)/shard_map/slice | solution.py:12
  7.0 0.7 multiply_add_fusion
  7.7 0.1 add_multiply_fusion
  7.8 0.0 collective-permute-done
  7.8 0.0 copy-done
  7.8 0.1 maximum_select_fusion
  8.0 13.4 %fusion.10 = f32[32,128,2,32]{1,3,2,0:T(8,128)S(1)} fusion(bf16[2,32,2048,1]{2,1,0,3:T(8,128)(2,1)S(1)} %bitcast.53, s32[2048]{0:T(1024)S(1)} %get-tuple-element.5, s32[]{:T(128)} %bitcast.3, s32[32,128]{1,0:T(8,128)S(1)} %add_multiply_fusion), kind=kOutput, calls=%fused_computation.16 | convolution fusion | flops 1166016512 | bytes 1335300 | tf_op jit(solution)/shard_map/cra,apj->pcrj/dot_general | solution.py:67
  21.4 13.5 %fusion.18 = f32[32,128,2,32]{1,3,2,0:T(8,128)S(1)} fusion(f32[32,128,2,32]{1,3,2,0:T(8,128)S(1)} %fusion.10, bf16[2,32,2048,1]{2,1,0,3:T(8,128)(2,1)S(1)} %bitcast.52, s32[]{:T(128)} %bitcast.3, s32[32,128]{1,0:T(8,128)S(1)} %add_multiply_fusion, s32[2048]{0:T(1024)S(1)} %get-tuple-element.4), kind=kOutput, calls=%fused_computation.22 | convolution fusion | flops 1166278656 | bytes 2383876 | tf_op jit(solution)/shard_map/cra,apj->pcrj/dot_general | solution.py:67
  34.9 40.9 %all_to_all.5 = f32[64,32,128]{2,1,0:T(8,128)S(1)} all-to-all(f32[64,32,128]{2,1,0:T(8,128)S(1)} %bitcast.51), channel_id=1, replica_groups=mesh['param'=32,'ey'=8,'ec'=2] {'param','ec'}, dimensions={0} | all-to-all | bytes 2097152 | tf_op jit(solution)/shard_map/all_to_all | solution.py:75
  75.8 0.0 copy-start.1
  75.8 0.1 reduce_sum.27
  75.9 0.1 fusion.23
  76.0 19.0 %all_gather.3 = f32[512,256]{1,0:T(8,128)S(1)} all-gather(f32[32,256]{1,0:T(8,128)S(1)} %copy_bitcast_fusion), channel_id=1, replica_groups=mesh['param'=32,'ey'=8,'ec'=2] {'ey','ec'}, dimensions={0}, use_global_device_ids=true | all-gather | bytes 557056 | tf_op jit(solution)/shard_map/all_gather | solution.py:78
  95.0 0.0 copy-done.1
  95.0 0.7 multiply_reduce_fusion
  95.7 0.2 convolution_bitcast_fusion
  96.0 0.1 concatenate.11
  96.1 3.3 %collective-permute-start.1 = (f32[8480]{0:T(1024)S(1)}, f32[8480]{0:T(1024)S(1)}, u32[]{:S(2)}, u32[]{:S(2)}) collective-permute-start(f32[8480]{0:T(1024)S(1)} %concatenate.11), channel_id=1, source_target_pairs={{0,16},{16,0},{32,48},{48,32},{64,80},{80,64},{96,112},{112,96},{1... | collective-permute-start | bytes 101768 | tf_op jit(solution)/shard_map/ppermute | solution.py:33
  99.3 2.6 %collective-permute-done.1 = f32[8480]{0:T(1024)S(1)} collective-permute-done((f32[8480]{0:T(1024)S(1)}, f32[8480]{0:T(1024)S(1)}, u32[]{:S(2)}, u32[]{:S(2)}) %collective-permute-start.1) | collective-permute-done | bytes 33952 | tf_op jit(solution)/shard_map/ppermute | solution.py:33
  101.9 4.8 %collective-permute-start.2 = (f32[8480]{0:T(1024)S(1)}, f32[8480]{0:T(1024)S(1)}, u32[]{:S(2)}, u32[]{:S(2)}) collective-permute-start(f32[8480]{0:T(1024)S(1)} %add.124), channel_id=1, source_target_pairs={{0,32},{16,48},{32,0},{48,16},{64,96},{80,112},{96,64},{112,80},{1... | collective-permute-start | bytes 101768 | tf_op jit(solution)/shard_map/ppermute | solution.py:33
  106.7 1.9 %collective-permute-done.2 = f32[8480]{0:T(1024)S(1)} collective-permute-done((f32[8480]{0:T(1024)S(1)}, f32[8480]{0:T(1024)S(1)}, u32[]{:S(2)}, u32[]{:S(2)}) %collective-permute-start.2) | collective-permute-done | bytes 33952 | tf_op jit(solution)/shard_map/ppermute | solution.py:33
  108.7 5.2 %collective-permute-start.3 = (f32[8480]{0:T(1024)S(1)}, f32[8480]{0:T(1024)S(1)}, u32[]{:S(2)}, u32[]{:S(2)}) collective-permute-start(f32[8480]{0:T(1024)S(1)} %add.125), channel_id=1, source_target_pairs={{0,64},{16,80},{32,96},{48,112},{64,0},{80,16},{96,32},{112,48},{1... | collective-permute-start | bytes 101768 | tf_op jit(solution)/shard_map/ppermute | solution.py:33
  113.9 4.5 %collective-permute-done.3 = f32[8480]{0:T(1024)S(1)} collective-permute-done((f32[8480]{0:T(1024)S(1)}, f32[8480]{0:T(1024)S(1)}, u32[]{:S(2)}, u32[]{:S(2)}) %collective-permute-start.3) | collective-permute-done | bytes 33952 | tf_op jit(solution)/shard_map/ppermute | solution.py:33
  118.4 3.4 %collective-permute-start.4 = (f32[8480]{0:T(1024)S(1)}, f32[8480]{0:T(1024)S(1)}, u32[]{:S(2)}, u32[]{:S(2)}) collective-permute-start(f32[8480]{0:T(1024)S(1)} %add.126), channel_id=1, source_target_pairs={{0,128},{16,144},{32,160},{48,176},{64,192},{80,208},{96,224},{112... | collective-permute-start | bytes 101768 | tf_op jit(solution)/shard_map/ppermute | solution.py:33
  121.9 2.4 %collective-permute-done.4 = f32[8480]{0:T(1024)S(1)} collective-permute-done((f32[8480]{0:T(1024)S(1)}, f32[8480]{0:T(1024)S(1)}, u32[]{:S(2)}, u32[]{:S(2)}) %collective-permute-start.4) | collective-permute-done | bytes 33952 | tf_op jit(solution)/shard_map/ppermute | solution.py:33
  124.3 4.0 %collective-permute-start.5 = (f32[8480]{0:T(1024)S(1)}, f32[8480]{0:T(1024)S(1)}, u32[]{:S(2)}, u32[]{:S(2)}) collective-permute-start(f32[8480]{0:T(1024)S(1)} %add.127), channel_id=1, source_target_pairs={{0,256},{16,272},{32,288},{48,304},{64,320},{80,336},{96,352},{112... | collective-permute-start | bytes 101768 | tf_op jit(solution)/shard_map/ppermute | solution.py:33
  128.3 3.3 %collective-permute-done.5 = f32[8480]{0:T(1024)S(1)} collective-permute-done((f32[8480]{0:T(1024)S(1)}, f32[8480]{0:T(1024)S(1)}, u32[]{:S(2)}, u32[]{:S(2)}) %collective-permute-start.5) | collective-permute-done | bytes 33952 | tf_op jit(solution)/shard_map/ppermute | solution.py:33
  131.6 0.1 fusion.25
  131.7 0.7 multiply_multiply_fusion
  (14 shorter events, 0.2 us)
Async XLA Ops:
  0.6 7.2 %copy-start = (bf16[32,4096]{1,0:T(8,128)(2,1)S(1)}, bf16[32,4096]{1,0:T(8,128)(2,1)}, u32[]{:S(2)}) copy-start(bf16[32,4096]{1,0:T(8,128)(2,1)} %param.3) | copy-start | bytes 786436
  1.7 6.1 %collective-permute-start = (f32[32,4096]{1,0:T(8,128)S(1)}, f32[32,4096]{1,0:T(8,128)S(1)}, u32[]{:S(2)}, u32[]{:S(2)}) collective-permute-start(f32[32,4096]{1,0:T(8,128)S(1)} %convert_element_type.10), channel_id=1, source_target_pairs={{0,1},{1,0},{2,3},{3,2},{4,5},{5,4},{6,7},{7,6},{8,9},{9,8},{10,11... | collective-permute-start | bytes 1572872 | tf_op jit(solution)/shard_map/ppermute | solution.py:50
  75.8 19.2 %copy-start.1 = (s32[256]{0:T(256)S(1)}, s32[256]{0:T(256)}, u32[]{:S(2)}) copy-start(s32[256]{0:T(256)} %param.5) | copy-start | bytes 3076
  96.1 5.8 %collective-permute-start.1 = (f32[8480]{0:T(1024)S(1)}, f32[8480]{0:T(1024)S(1)}, u32[]{:S(2)}, u32[]{:S(2)}) collective-permute-start(f32[8480]{0:T(1024)S(1)} %concatenate.11), channel_id=1, source_target_pairs={{0,16},{16,0},{32,48},{48,32},{64,80},{80,64},{96,112},{112,96},{1... | collective-permute-start | bytes 101768 | tf_op jit(solution)/shard_map/ppermute | solution.py:33
  101.9 6.7 %collective-permute-start.2 = (f32[8480]{0:T(1024)S(1)}, f32[8480]{0:T(1024)S(1)}, u32[]{:S(2)}, u32[]{:S(2)}) collective-permute-start(f32[8480]{0:T(1024)S(1)} %add.124), channel_id=1, source_target_pairs={{0,32},{16,48},{32,0},{48,16},{64,96},{80,112},{96,64},{112,80},{1... | collective-permute-start | bytes 101768 | tf_op jit(solution)/shard_map/ppermute | solution.py:33
  108.7 9.7 %collective-permute-start.3 = (f32[8480]{0:T(1024)S(1)}, f32[8480]{0:T(1024)S(1)}, u32[]{:S(2)}, u32[]{:S(2)}) collective-permute-start(f32[8480]{0:T(1024)S(1)} %add.125), channel_id=1, source_target_pairs={{0,64},{16,80},{32,96},{48,112},{64,0},{80,16},{96,32},{112,48},{1... | collective-permute-start | bytes 101768 | tf_op jit(solution)/shard_map/ppermute | solution.py:33
  118.4 5.8 %collective-permute-start.4 = (f32[8480]{0:T(1024)S(1)}, f32[8480]{0:T(1024)S(1)}, u32[]{:S(2)}, u32[]{:S(2)}) collective-permute-start(f32[8480]{0:T(1024)S(1)} %add.126), channel_id=1, source_target_pairs={{0,128},{16,144},{32,160},{48,176},{64,192},{80,208},{96,224},{112... | collective-permute-start | bytes 101768 | tf_op jit(solution)/shard_map/ppermute | solution.py:33
  124.3 7.3 %collective-permute-start.5 = (f32[8480]{0:T(1024)S(1)}, f32[8480]{0:T(1024)S(1)}, u32[]{:S(2)}, u32[]{:S(2)}) collective-permute-start(f32[8480]{0:T(1024)S(1)} %add.127), channel_id=1, source_target_pairs={{0,256},{16,272},{32,288},{48,304},{64,320},{80,336},{96,352},{112... | collective-permute-start | bytes 101768 | tf_op jit(solution)/shard_map/ppermute | solution.py:33
where the time goes:
time: 133 us; the launch traced here: 132 us
  blocking collectives  59.9 us (45%)
  matrix products  27.9 us (21%)
  starting transfers between devices  22.7 us (17%)
  waiting for transfers between devices  14.7 us (11%)
  other arithmetic  2.91 us (2%)
  between operations  2.7 us (2%)
  local copies, waits for them, and re-layouts  1.65 us (1%)
    all_to_all x1, blocking collectives, local(): blocks = lax.all_to_all(blocks, ('param', 'ec'), 0, 0, tiled=True)  40.9 us
    dot_general x2, matrix products, local(): jnp.einsum('cra,apj->pcrj', gradient_slab.reshape(2, resident_example, ro...  27 us
    ppermute x5, starting transfers between devices, butterfly_sum(): values = values + lax.ppermute(values, axis, pairs)  20.8 us
    all_gather x1, blocking collectives, local(): pool_rows = lax.all_gather(projected, ('ey', 'ec'), axis=0, tiled=True)  19 us
    ppermute x5, waiting for transfers between devices, butterfly_sum(): values = values + lax.ppermute(values, axis, pairs)  14.7 us
  transfers between devices with their start and end apart: 6, of which 5 were waited for; matrix products, arithmetic and copies ran while one was open for 2% of the time, Pallas kernels for 0%

commit v1 on v0

--- a/solution.py
+++ b/solution.py
@@ -75,7 +75,10 @@
     blocks = lax.all_to_all(blocks, ("param", "ec"), 0, 0, tiled=True)
     blocks = jnp.sum(blocks.reshape(param_count, 2, resident_example, half_width), axis=0)
     projected = jnp.transpose(blocks, (1, 0, 2)).reshape(resident_example, col_width)
-    pool_rows = lax.all_gather(projected, ("ey", "ec"), axis=0, tiled=True)
+    pool_rows = jnp.concatenate(
+        lax.all_to_all(jnp.stack([projected] * lax.axis_size(("ey", "ec"))), ("ey", "ec"), 0, 0),
+        axis=0,
+    )
     picks = (target_indices[:, None] == lax.iota(jnp.int32, pool_rows.shape[0])[None, :]).astype(
         jnp.float32
     )

time: 133 us -> 140 us (1.053)
  waiting for transfers between devices: 14.7 us -> 36.2 us
  blocking collectives: 59.9 us -> 40.9 us
  starting transfers between devices: 22.7 us -> 26.5 us
    all_gather x1 -> x0, blocking collectives: 19 us -> none  [local(): pool_rows = lax.all_gather(projected, ('ey', 'ec'), axis=0, tiled=True)]
    all_to_all x0 -> x1, waiting for transfers between devices: none -> 15.9 us  [local(): lax.all_to_all(jnp.stack([projected] * lax.axis_size(('ey', 'ec'))), ('ey...]
    all_to_all x0 -> x1, starting transfers between devices: none -> 8.22 us  [local(): lax.all_to_all(jnp.stack([projected] * lax.axis_size(('ey', 'ec'))), ('ey...]
    ppermute x5, waiting for transfers between devices: 14.7 us -> 20.3 us  [butterfly_sum(): values = values + lax.ppermute(values, axis, pairs)]
    ppermute x5, starting transfers between devices: 20.8 us -> 16.4 us  [butterfly_sum(): values = values + lax.ppermute(values, axis, pairs)]
  transfers between devices with their start and end apart: 6 -> 7, of which waited for: 5 -> 6; matrix products, arithmetic and copies ran while one was open for 2% -> 2% of each run, Pallas kernels for 0% -> 0%
where the time goes in v1:
time: 140 us
  blocking collectives  40.9 us (29%)
  waiting for transfers between devices  36.2 us (26%)
  matrix products  27.9 us (20%)
  starting transfers between devices  26.5 us (19%)
  other arithmetic  2.91 us (2%)
  between operations  2.71 us (2%)
  local copies, waits for them, and re-layouts  2.48 us (2%)
    all_to_all x1, blocking collectives, local(): blocks = lax.all_to_all(blocks, ('param', 'ec'), 0, 0, tiled=True)  40.9 us
    dot_general x2, matrix products, local(): jnp.einsum('cra,apj->pcrj', gradient_slab.reshape(2, resident_example, ro...  27 us
    ppermute x5, waiting for transfers between devices, butterfly_sum(): values = values + lax.ppermute(values, axis, pairs)  20.3 us
    ppermute x5, starting transfers between devices, butterfly_sum(): values = values + lax.ppermute(values, axis, pairs)  16.4 us
    all_to_all x1, waiting for transfers between devices, local(): lax.all_to_all(jnp.stack([projected] * lax.axis_size(('ey', 'ec'))), ('ey...  15.9 us
    all_to_all x1, starting transfers between devices, local(): lax.all_to_all(jnp.stack([projected] * lax.axis_size(('ey', 'ec'))), ('ey...  8.22 us
  transfers between devices with their start and end apart: 7, of which 6 were waited for; matrix products, arithmetic and copies ran while one was open for 2% of the time, Pallas kernels for 0%

profile of v1, /device:TPU:2, one launch (start us, length us, event | category | flops | bytes accessed | tf_op | source)
XLA Modules:
  0.0 139.6 jit_solution(9576021797102325108)
XLA Ops:
  0.6 0.0 copy-start
  0.6 1.1 convert_element_type.10
  1.7 1.9 %collective-permute-start = (f32[32,4096]{1,0:T(8,128)S(1)}, f32[32,4096]{1,0:T(8,128)S(1)}, u32[]{:S(2)}, u32[]{:S(2)}) collective-permute-start(f32[32,4096]{1,0:T(8,128)S(1)} %convert_element_type.10), channel_id=1, source_target_pairs={{0,1},{1,0},{2,3},{3,2},{4,5},{5,4},{6,7},{7,6},{8,9},{9,8},{10,11... | collective-permute-start | bytes 1572872 | tf_op jit(solution)/shard_map/ppermute | solution.py:50
  3.6 1.5 %fusion.42 = (s32[1]{0:T(128)}, s32[1]{0:T(128)}, s32[1]{0:T(128)}, s32[1]{0:T(128)}) fusion(s32[4]{0:T(128)} %param.4), kind=kLoop, calls=%fused_computation.58 | loop fusion | bytes 32 | tf_op jit(solution)/shard_map/slice | solution.py:12
  7.0 0.7 multiply_add_fusion
  7.7 0.1 add_multiply_fusion
  7.7 0.0 collective-permute-done
  7.8 0.0 copy-done
  7.8 0.1 maximum_select_fusion
  7.9 13.4 %fusion.10 = f32[32,128,2,32]{1,3,2,0:T(8,128)S(1)} fusion(bf16[2,32,2048,1]{2,1,0,3:T(8,128)(2,1)S(1)} %bitcast.55, s32[2048]{0:T(1024)S(1)} %get-tuple-element.5, s32[]{:T(128)} %bitcast.3, s32[32,128]{1,0:T(8,128)S(1)} %add_multiply_fusion), kind=kOutput, calls=%fused_computation.16 | convolution fusion | flops 1166016512 | bytes 1335300 | tf_op jit(solution)/shard_map/cra,apj->pcrj/dot_general | solution.py:67
  21.4 13.5 %fusion.18 = f32[32,128,2,32]{1,3,2,0:T(8,128)S(1)} fusion(f32[32,128,2,32]{1,3,2,0:T(8,128)S(1)} %fusion.10, bf16[2,32,2048,1]{2,1,0,3:T(8,128)(2,1)S(1)} %bitcast.54, s32[]{:T(128)} %bitcast.3, s32[32,128]{1,0:T(8,128)S(1)} %add_multiply_fusion, s32[2048]{0:T(1024)S(1)} %get-tuple-element.4), kind=kOutput, calls=%fused_computation.22 | convolution fusion | flops 1166278656 | bytes 2383876 | tf_op jit(solution)/shard_map/cra,apj->pcrj/dot_general | solution.py:67
  34.9 40.9 %all_to_all.10 = f32[64,32,128]{2,1,0:T(8,128)S(1)} all-to-all(f32[64,32,128]{2,1,0:T(8,128)S(1)} %bitcast.53), channel_id=1, replica_groups=mesh['param'=32,'ey'=8,'ec'=2] {'param','ec'}, dimensions={0} | all-to-all | bytes 2097152 | tf_op jit(solution)/shard_map/all_to_all | solution.py:75
  75.8 0.1 reduce_sum.27
  75.9 0.0 copy-start.1
  75.9 0.8 stack.3
  76.7 8.2 %all-to-all-start.1 = ((f32[16,32,256]{2,1,0:T(8,128)}), f32[16,32,256]{2,1,0:T(8,128)S(1)}, u32[]{:S(2)}, u32[]{:S(2)}) async-start(f32[16,32,256]{2,1,0:T(8,128)} %stack.3), calls=%async_computation.1 | async-start | bytes 1048576 | tf_op jit(solution)/shard_map/all_to_all | solution.py:79
  85.0 0.1 fusion.23
  85.1 15.9 %all-to-all-done.1 = f32[16,32,256]{2,1,0:T(8,128)S(1)} async-done(((f32[16,32,256]{2,1,0:T(8,128)}), f32[16,32,256]{2,1,0:T(8,128)S(1)}, u32[]{:S(2)}, u32[]{:S(2)}) %all-to-all-start.1) | async-done | bytes 524320 | tf_op jit(solution)/shard_map/all_to_all | solution.py:79
  101.0 0.0 copy-done.1
  101.0 0.7 multiply_reduce_fusion
  101.7 0.2 convolution_bitcast_fusion
  101.9 0.1 concatenate.11
  102.0 2.5 %collective-permute-start.1 = (f32[8480]{0:T(1024)S(1)}, f32[8480]{0:T(1024)S(1)}, u32[]{:S(2)}, u32[]{:S(2)}) collective-permute-start(f32[8480]{0:T(1024)S(1)} %concatenate.11), channel_id=1, source_target_pairs={{0,16},{16,0},{32,48},{48,32},{64,80},{80,64},{96,112},{112,96},{1... | collective-permute-start | bytes 101768 | tf_op jit(solution)/shard_map/ppermute | solution.py:33
  104.5 3.4 %collective-permute-done.1 = f32[8480]{0:T(1024)S(1)} collective-permute-done((f32[8480]{0:T(1024)S(1)}, f32[8480]{0:T(1024)S(1)}, u32[]{:S(2)}, u32[]{:S(2)}) %collective-permute-start.1) | collective-permute-done | bytes 33952 | tf_op jit(solution)/shard_map/ppermute | solution.py:33
  107.9 3.8 %collective-permute-start.2 = (f32[8480]{0:T(1024)S(1)}, f32[8480]{0:T(1024)S(1)}, u32[]{:S(2)}, u32[]{:S(2)}) collective-permute-start(f32[8480]{0:T(1024)S(1)} %add.124), channel_id=1, source_target_pairs={{0,32},{16,48},{32,0},{48,16},{64,96},{80,112},{96,64},{112,80},{1... | collective-permute-start | bytes 101768 | tf_op jit(solution)/shard_map/ppermute | solution.py:33
  111.7 3.7 %collective-permute-done.2 = f32[8480]{0:T(1024)S(1)} collective-permute-done((f32[8480]{0:T(1024)S(1)}, f32[8480]{0:T(1024)S(1)}, u32[]{:S(2)}, u32[]{:S(2)}) %collective-permute-start.2) | collective-permute-done | bytes 33952 | tf_op jit(solution)/shard_map/ppermute | solution.py:33
  115.4 3.8 %collective-permute-start.3 = (f32[8480]{0:T(1024)S(1)}, f32[8480]{0:T(1024)S(1)}, u32[]{:S(2)}, u32[]{:S(2)}) collective-permute-start(f32[8480]{0:T(1024)S(1)} %add.125), channel_id=1, source_target_pairs={{0,64},{16,80},{32,96},{48,112},{64,0},{80,16},{96,32},{112,48},{1... | collective-permute-start | bytes 101768 | tf_op jit(solution)/shard_map/ppermute | solution.py:33
  119.2 6.3 %collective-permute-done.3 = f32[8480]{0:T(1024)S(1)} collective-permute-done((f32[8480]{0:T(1024)S(1)}, f32[8480]{0:T(1024)S(1)}, u32[]{:S(2)}, u32[]{:S(2)}) %collective-permute-start.3) | collective-permute-done | bytes 33952 | tf_op jit(solution)/shard_map/ppermute | solution.py:33
  125.5 2.5 %collective-permute-start.4 = (f32[8480]{0:T(1024)S(1)}, f32[8480]{0:T(1024)S(1)}, u32[]{:S(2)}, u32[]{:S(2)}) collective-permute-start(f32[8480]{0:T(1024)S(1)} %add.126), channel_id=1, source_target_pairs={{0,128},{16,144},{32,160},{48,176},{64,192},{80,208},{96,224},{112... | collective-permute-start | bytes 101768 | tf_op jit(solution)/shard_map/ppermute | solution.py:33
  128.0 3.4 %collective-permute-done.4 = f32[8480]{0:T(1024)S(1)} collective-permute-done((f32[8480]{0:T(1024)S(1)}, f32[8480]{0:T(1024)S(1)}, u32[]{:S(2)}, u32[]{:S(2)}) %collective-permute-start.4) | collective-permute-done | bytes 33952 | tf_op jit(solution)/shard_map/ppermute | solution.py:33
  131.4 3.8 %collective-permute-start.5 = (f32[8480]{0:T(1024)S(1)}, f32[8480]{0:T(1024)S(1)}, u32[]{:S(2)}, u32[]{:S(2)}) collective-permute-start(f32[8480]{0:T(1024)S(1)} %add.127), channel_id=1, source_target_pairs={{0,256},{16,272},{32,288},{48,304},{64,320},{80,336},{96,352},{112... | collective-permute-start | bytes 101768 | tf_op jit(solution)/shard_map/ppermute | solution.py:33
  135.2 3.5 %collective-permute-done.5 = f32[8480]{0:T(1024)S(1)} collective-permute-done((f32[8480]{0:T(1024)S(1)}, f32[8480]{0:T(1024)S(1)}, u32[]{:S(2)}, u32[]{:S(2)}) %collective-permute-start.5) | collective-permute-done | bytes 33952 | tf_op jit(solution)/shard_map/ppermute | solution.py:33
  138.7 0.1 fusion.25
  138.9 0.7 multiply_multiply_fusion
  (14 shorter events, 0.2 us)
Async XLA Ops:
  0.6 7.2 %copy-start = (bf16[32,4096]{1,0:T(8,128)(2,1)S(1)}, bf16[32,4096]{1,0:T(8,128)(2,1)}, u32[]{:S(2)}) copy-start(bf16[32,4096]{1,0:T(8,128)(2,1)} %param.3) | copy-start | bytes 786436
  1.7 6.1 %collective-permute-start = (f32[32,4096]{1,0:T(8,128)S(1)}, f32[32,4096]{1,0:T(8,128)S(1)}, u32[]{:S(2)}, u32[]{:S(2)}) collective-permute-start(f32[32,4096]{1,0:T(8,128)S(1)} %convert_element_type.10), channel_id=1, source_target_pairs={{0,1},{1,0},{2,3},{3,2},{4,5},{5,4},{6,7},{7,6},{8,9},{9,8},{10,11... | collective-permute-start | bytes 1572872 | tf_op jit(solution)/shard_map/ppermute | solution.py:50
  75.9 25.1 %copy-start.1 = (s32[256]{0:T(256)S(1)}, s32[256]{0:T(256)}, u32[]{:S(2)}) copy-start(s32[256]{0:T(256)} %param.5) | copy-start | bytes 3076
  76.7 24.3 %all-to-all-start.1 = ((f32[16,32,256]{2,1,0:T(8,128)}), f32[16,32,256]{2,1,0:T(8,128)S(1)}, u32[]{:S(2)}, u32[]{:S(2)}) async-start(f32[16,32,256]{2,1,0:T(8,128)} %stack.3), calls=%async_computation.1 | async-start | bytes 1048576 | tf_op jit(solution)/shard_map/all_to_all | solution.py:79
  102.0 5.8 %collective-permute-start.1 = (f32[8480]{0:T(1024)S(1)}, f32[8480]{0:T(1024)S(1)}, u32[]{:S(2)}, u32[]{:S(2)}) collective-permute-start(f32[8480]{0:T(1024)S(1)} %concatenate.11), channel_id=1, source_target_pairs={{0,16},{16,0},{32,48},{48,32},{64,80},{80,64},{96,112},{112,96},{1... | collective-permute-start | bytes 101768 | tf_op jit(solution)/shard_map/ppermute | solution.py:33
  107.9 7.5 %collective-permute-start.2 = (f32[8480]{0:T(1024)S(1)}, f32[8480]{0:T(1024)S(1)}, u32[]{:S(2)}, u32[]{:S(2)}) collective-permute-start(f32[8480]{0:T(1024)S(1)} %add.124), channel_id=1, source_target_pairs={{0,32},{16,48},{32,0},{48,16},{64,96},{80,112},{96,64},{112,80},{1... | collective-permute-start | bytes 101768 | tf_op jit(solution)/shard_map/ppermute | solution.py:33
  115.4 10.1 %collective-permute-start.3 = (f32[8480]{0:T(1024)S(1)}, f32[8480]{0:T(1024)S(1)}, u32[]{:S(2)}, u32[]{:S(2)}) collective-permute-start(f32[8480]{0:T(1024)S(1)} %add.125), channel_id=1, source_target_pairs={{0,64},{16,80},{32,96},{48,112},{64,0},{80,16},{96,32},{112,48},{1... | collective-permute-start | bytes 101768 | tf_op jit(solution)/shard_map/ppermute | solution.py:33
  125.5 5.8 %collective-permute-start.4 = (f32[8480]{0:T(1024)S(1)}, f32[8480]{0:T(1024)S(1)}, u32[]{:S(2)}, u32[]{:S(2)}) collective-permute-start(f32[8480]{0:T(1024)S(1)} %add.126), channel_id=1, source_target_pairs={{0,128},{16,144},{32,160},{48,176},{64,192},{80,208},{96,224},{112... | collective-permute-start | bytes 101768 | tf_op jit(solution)/shard_map/ppermute | solution.py:33
  131.4 7.3 %collective-permute-start.5 = (f32[8480]{0:T(1024)S(1)}, f32[8480]{0:T(1024)S(1)}, u32[]{:S(2)}, u32[]{:S(2)}) collective-permute-start(f32[8480]{0:T(1024)S(1)} %add.127), channel_id=1, source_target_pairs={{0,256},{16,272},{32,288},{48,304},{64,320},{80,336},{96,352},{112... | collective-permute-start | bytes 101768 | tf_op jit(solution)/shard_map/ppermute | solution.py:33
